TPU v7x, 32 devices: a whole 2x2x4 slice. The times are simulated.
32 devices in a mesh: groups: 2 (over y), dp: 4 (over z), tensor: 2 (over x), layer: 2 (over core).
Axes of the slice: x: 2, y: 2, z: 4, core: 2. Of those that a mesh axis runs over, the one named last changes fastest.
Arguments:
- hidden_in: bfloat16 [2, 8, 512, 14336], P('layer', ('groups', 'dp'), None, 'tensor'), parts along dimension 1, may hold values from -6 to 6
- out_grad: bfloat16 [2, 8, 512, 4096], P('layer', ('groups', 'dp'), 'tensor'), parts along dimension 1, may hold values from -6 to 6
- proj_in: bfloat16 [2, 14336, 64], P('layer', 'tensor'), may hold values from -0.046875 to 0.046875
- proj_out: bfloat16 [2, 4096, 64], P('layer'), may hold values from -0.09375 to 0.09375
- query_grads: bfloat16 [2, 1024, 4096], P('layer', 'dp', 'tensor'), may hold values from -1.5 to 1.5
- lengths: int32 [8], P(('groups', 'dp')), parts along dimension 0, may hold values from 128 to 512, as said below
- query_decision: int32 [1024], P('dp'), may hold values from 0 to 1023
Outputs:
- influence: float32 [8, 1024], P(('groups', 'dp')), parts along dimension 0
There are 2 independent parts, one for each index of `groups`. A program takes and returns all parts, laid end to end along the dimension named above; an argument that names none is the same for every part. Nothing has to cross between parts.
Inputs may be any that keep to these rules, and one draw needn't show every extreme that they name: `lengths`: in each part one transcript has all 512 tokens live and another has exactly 128.
All inputs are finite; a program needn't handle non-finite values.
Results may differ from a plain program's by a relative error of at most 0.004.
Values may be sent and summed in bfloat16 or wider, within the bound.
No kernel may reach another device: no remote copies, remote signals or barrier semaphores. Data moves between devices by JAX's collectives and lax.ppermute only.
A program may use at most 64 MiB of HBM per device.

v0:
```python
import jax
import jax.numpy as jnp
from jax import lax
from jax.sharding import PartitionSpec as P

DECISIONS = 1024


def decision_table(decisions):
    return (decisions[:, None] == jnp.arange(DECISIONS, dtype=jnp.int32)[None, :]).astype(
        jnp.float32
    )


def body(hidden_in, out_grad, proj_in, proj_out, query_grads, lengths, query_decision):
    hidden_rows = hidden_in[0]
    grad_rows = out_grad[0]
    side_hidden = proj_in[0]
    side_width = proj_out[0]
    query_rows = query_grads[0]
    ex_count = hidden_rows.shape[0]
    seq_shard = grad_rows.shape[1]
    first_pos = lax.axis_index("tensor") * seq_shard
    positions = first_pos + jnp.arange(seq_shard, dtype=jnp.int32)
    live_tokens = (positions[None, :] < lengths[:, None]).astype(jnp.float32)
    right = jnp.einsum("etd,dp->etp", grad_rows, side_width, preferred_element_type=jnp.float32)
    right = (right * live_tokens[:, :, None]).astype(jnp.bfloat16)
    left = jnp.einsum("etf,fp->etp", hidden_rows, side_hidden, preferred_element_type=jnp.float32)
    left_own = lax.psum_scatter(left, "tensor", scatter_dimension=1, tiled=True)
    partial_value = jnp.einsum(
        "etp,etq->epq", left_own, right.astype(jnp.float32), precision=lax.Precision.HIGHEST
    )
    partial_value = partial_value / lengths.astype(jnp.float32)[:, None, None]
    grad_part = lax.psum_scatter(partial_value, "tensor", scatter_dimension=1, tiled=True)
    grad_flat = grad_part.reshape(ex_count, -1).astype(jnp.bfloat16)
    block_rows = lax.all_gather(query_rows, "dp", axis=0, tiled=True)
    block_decisions = lax.all_gather(query_decision, "dp", axis=0, tiled=True)
    scores = jnp.einsum("ek,qk->eq", grad_flat, block_rows, preferred_element_type=jnp.float32)
    partial_dec = jnp.dot(scores, decision_table(block_decisions), precision=lax.Precision.HIGHEST)
    result = lax.psum(partial_dec, ("tensor", "layer"))
    return result


def solution(mesh):
    in_specs = (
        P("layer", ("groups", "dp"), None, "tensor"),
        P("layer", ("groups", "dp"), "tensor", None),
        P("layer", "tensor", None),
        P("layer", None, None),
        P("layer", "dp", "tensor"),
        P(("groups", "dp")),
        P("dp"),
    )
    out_specs = P(("groups", "dp"), None)
    return jax.shard_map(body, mesh=mesh, in_specs=in_specs, out_specs=out_specs, check_vma=False)
```

profile of v0, /device:TPU:0, one launch (start us, length us, event | category | flops | bytes accessed | tf_op | source)
XLA Modules:
  0.0 130.6 jit_solution(11717772726066423702)
XLA Ops:
  7.4 0.0 copy-start
  7.4 0.0 copy-start.2
  7.4 0.0 copy-start.1
  7.4 0.0 reduce-scatter.3.cloned.1.call-start
  7.4 6.4 %fusion.11 = f32[1,512,64]{1,2,0:T(8,128)} fusion(bf16[1,1,512,7168]{3,2,1,0:T(8,128)(2,1)} %param.7, bf16[1,7168,64]{1,2,0:T(8,128)(2,1)} %param.9), kind=kOutput, calls=%fused_computation.10 | convolution fusion | flops 469762048 | bytes 8388608 | tf_op jit(solution)/shard_map/etf,fp->etp/dot_general | solution.py:28
  13.8 0.0 reduce-scatter.3.cloned.1.call-update
  13.8 0.0 reduce-scatter.5.cloned.1.call-start
  14.5 0.0 copy-done
  14.5 0.0 copy-done.2
  14.6 0.7 fusion.14
  15.2 11.8 %reduce-scatter.3.cloned.1.call-done = f32[1,256,64]{1,2,0:T(8,128)} async-done(((f32[1,512,64]{1,2,0:T(8,128)}), f32[1,256,64]{1,2,0:T(8,128)}) %reduce-scatter.3.cloned.1.call-update) | async-done | bytes 65552 | tf_op jit(solution)/shard_map/reduce_scatter | solution.py:29
  27.1 1.6 %fusion.17 = f32[1,64,64]{2,1,0:T(8,128)} fusion(bf16[256,64]{1,0:T(8,128)(2,1)S(1)} %fusion.14, f32[1,256,64]{1,2,0:T(8,128)} %reduce-scatter.3.cloned.1.call-done, f32[]{:T(128)} %bitcast.7), kind=kOutput, calls=%fused_computation.13 | convolution fusion | flops 12587008 | bytes 114692 | tf_op jit(solution)/shard_map/etp,etq->epq/dot_general | solution.py:30
  28.7 0.0 reduce-scatter.5.cloned.1.call-update
  28.7 0.0 all-gather.4.cloned.1.call-start
  28.7 0.5 all-gather.4.cloned.1.call-update
  29.3 0.0 copy-done.1
  29.3 10.9 %all-gather.1 = s32[4,1,256]{2,1,0:T(1,128)S(1)} all-gather(s32[1,1,256]{2,1,0:T(1,128)S(1)} %bitcast.43), channel_id=1, replica_groups=mesh['groups'=2,'dp'=4,'tensor'=2,'layer'=2] {'dp'}, dimensions={0}, use_global_device_ids=true | all-gather | bytes 5120 | tf_op jit(solution)/shard_map/all_gather | solution.py:37
  40.2 0.0 reduce-scatter.5.cloned.1.call-done
  40.2 0.7 convert_element_type.30
  40.9 0.1 reshape.54
  41.0 70.4 %all-gather.4.cloned.1.call-done = bf16[1,1024,2048]{2,1,0:T(8,128)(2,1)} async-done(((bf16[1,256,2048]{2,1,0:T(8,128)(2,1)}), bf16[1,1024,2048]{2,1,0:T(8,128)(2,1)}) %all-gather.4.cloned.1.call-update) | async-done | bytes 4194320 | tf_op jit(solution)/shard_map/all_gather | solution.py:36
  111.4 3.4 %fusion.18 = f32[1024,1]{0,1:T(1,128)S(1)} fusion(bf16[2048,1]{0,1:T(2,128)(2,1)S(1)} %reshape.54, bf16[1,1024,2048]{2,1,0:T(8,128)(2,1)} %all-gather.4.cloned.1.call-done), kind=kOutput, calls=%fused_computation.14 | convolution fusion | flops 4194304 | bytes 4202496 | tf_op jit(solution)/shard_map/ek,qk->eq/dot_general | solution.py:38
  114.7 1.5 %fusion.4 = f32[1,1024]{1,0:T(1,128)S(1)} fusion(f32[1024,1]{0,1:T(1,128)S(1)} %fusion.18, s32[1024]{0:T(1024)S(1)} %bitcast.42), kind=kOutput, calls=%fused_computation.5 | convolution fusion | flops 13631488 | bytes 12288 | tf_op jit(solution)/shard_map/dot_general | solution.py:39
  116.2 7.0 %psum.7 = f32[1,1024]{1,0:T(1,128)} all-reduce(f32[1,1024]{1,0:T(1,128)S(1)} %fusion.4), channel_id=1, replica_groups=mesh['groups'=2,'dp'=4,'tensor'=2,'layer'=2] {'tensor','layer'}, use_global_device_ids=true, to_apply=%region_2.0 | all-reduce | flops 1024 | bytes 8192 | tf_op jit(solution)/shard_map/psum | solution.py:40
  (1 shorter events, 0.0 us)
Async XLA Ops:
  7.4 7.2 %copy-start = (bf16[1,1,256,4096]{3,2,1,0:T(8,128)(2,1)S(1)}, bf16[1,1,256,4096]{3,2,1,0:T(8,128)(2,1)}, u32[]{:S(2)}) copy-start(bf16[1,1,256,4096]{3,2,1,0:T(8,128)(2,1)} %param.8) | copy-start | bytes 6291460
  7.4 7.2 %copy-start.2 = (bf16[1,4096,64]{1,2,0:T(8,128)(2,1)S(1)}, bf16[1,4096,64]{1,2,0:T(8,128)(2,1)}, u32[]{:S(2)}) copy-start(bf16[1,4096,64]{1,2,0:T(8,128)(2,1)} %param.10) | copy-start | bytes 1572868
  7.4 21.9 %copy-start.1 = (s32[256]{0:T(256)S(1)}, s32[256]{0:T(256)}, u32[]{:S(2)}) copy-start(s32[256]{0:T(256)} %param.13) | copy-start | bytes 3076
  7.4 19.7 %reduce-scatter.3.cloned.1.call-start = ((), (), s32[]{:S(2)}) async-start(), calls=%async_computation.2 | async-start | bytes 196608 | tf_op jit(solution)/shard_map/reduce_scatter | solution.py:29
  13.8 26.4 %reduce-scatter.5.cloned.1.call-start = ((), (), s32[]{:S(2)}) async-start(), calls=%async_computation.3 | async-start | bytes 49152 | tf_op jit(solution)/shard_map/reduce_scatter | solution.py:34
  28.7 82.7 %all-gather.4.cloned.1.call-start = ((), (), s32[]{:S(2)}) async-start(), calls=%async_computation.4 | async-start | bytes 5242880 | tf_op jit(solution)/shard_map/all_gather | solution.py:36
Sparse Core Ops, SparseCore 0:
  13.9 13.0 reduce-scatter.2
  29.2 9.9 reduce-scatter.4
Sparse Core Ops, SparseCore 1:
  30.7 80.6 all-gather.3
where the time goes:
time: 131 us
  waiting for transfers between devices  82.7 us (63%)
  blocking collectives  17.9 us (14%)
  between operations  15.5 us (12%)
  matrix products  13.5 us (10%)
    all_gather x1, waiting for transfers between devices, body(): block_rows = lax.all_gather(query_rows, 'dp', axis=0, tiled=True)  70.4 us
    reduce_scatter x1, waiting for transfers between devices, body(): left_own = lax.psum_scatter(left, 'tensor', scatter_dimension=1, tiled=True)  11.8 us
    all_gather x1, blocking collectives, body(): block_decisions = lax.all_gather(query_decision, 'dp', axis=0, tiled=True)  10.9 us
    psum x1, blocking collectives, body(): result = lax.psum(partial_dec, ('tensor', 'layer'))  6.99 us
    dot_general x1, matrix products, body(): jnp.einsum('etf,fp->etp', hidden_rows, side_hidden, preferred_element_typ...  6.41 us
    dot_general x1, matrix products, body(): jnp.einsum('ek,qk->eq', grad_flat, block_rows, preferred_element_type=jnp...  3.37 us
  transfers between devices with their start and end apart: 3, of which 2 were waited for; matrix products, arithmetic and copies ran while one was open for 1% of the time, Pallas kernels for 0%

commit v1 on v0

--- a/solution.py
+++ b/solution.py
@@ -4,6 +4,28 @@
 from jax.sharding import PartitionSpec as P
 
 DECISIONS = 1024
+
+
+def joined_along(blocks, dim):
+    shape = list(blocks.shape[1:])
+    shape[dim] *= blocks.shape[0]
+    return jnp.moveaxis(blocks, 0, dim).reshape(shape)
+
+
+def gather_around(x, axis, dim):
+    size = lax.axis_size(axis)
+    pairs = [(i, (i + 1) % size) for i in range(size)]
+    back = [(b, a) for a, b in pairs]
+    lower, upper = ([], [])
+    for step in range(size - 1):
+        if step % 2 == 0:
+            lower.append(lax.ppermute(lower[-1] if lower else x, axis, pairs))
+        else:
+            upper.append(lax.ppermute(upper[-1] if upper else x, axis, back))
+    blocks = jnp.stack([*lower[::-1], x, *upper])
+    shift = lax.axis_index(axis) - len(lower)
+    blocks = blocks[(jnp.arange(size) - shift) % size]
+    return joined_along(blocks, dim)
 
 
 def decision_table(decisions):
@@ -33,7 +55,7 @@
     partial_value = partial_value / lengths.astype(jnp.float32)[:, None, None]
     grad_part = lax.psum_scatter(partial_value, "tensor", scatter_dimension=1, tiled=True)
     grad_flat = grad_part.reshape(ex_count, -1).astype(jnp.bfloat16)
-    block_rows = lax.all_gather(query_rows, "dp", axis=0, tiled=True)
+    block_rows = gather_around(query_rows, "dp", 0)
     block_decisions = lax.all_gather(query_decision, "dp", axis=0, tiled=True)
     scores = jnp.einsum("ek,qk->eq", grad_flat, block_rows, preferred_element_type=jnp.float32)
     partial_dec = jnp.dot(scores, decision_table(block_decisions), precision=lax.Precision.HIGHEST)

time: 131 us -> 114 us (0.87)
  waiting for transfers between devices: 82.7 us -> 53.2 us
  starting transfers between devices: 0.09 us -> 5.24 us
  local copies, waits for them, and re-layouts: 0.1 us -> 5.07 us
  other arithmetic: 0.73 us -> 4.32 us
  between operations: 15.5 us -> 14.1 us
    all_gather x1 -> x0, waiting for transfers between devices: 70.4 us -> none  [body(): block_rows = lax.all_gather(query_rows, 'dp', axis=0, tiled=True)]
    ppermute x0 -> x3, waiting for transfers between devices: none -> 24.3 us  [the longest x2 24.3 us: gather_around(): lower.append(lax.ppermute(lower[-1] if lower else x, axis, pairs))]
    reduce_scatter x1, waiting for transfers between devices: 11.8 us -> 28.8 us  [body(): left_own = lax.psum_scatter(left, 'tensor', scatter_dimension=1, tiled=True)]
    ppermute x0 -> x3, starting transfers between devices: none -> 5.2 us  [the longest x2 3.11 us: gather_around(): lower.append(lax.ppermute(lower[-1] if lower else x, axis, pairs))]
    gather x0 -> x1, local copies, waits for them, and re-layouts: none -> 4.97 us  [gather_around(): blocks = blocks[(jnp.arange(size) - shift) % size]]
    another operation x0 -> x1, other arithmetic: none -> 3.58 us  [gather_around(): blocks = jnp.stack([*lower[::-1], x, *upper])]
  transfers between devices with their start and end apart: 3 -> 5, of which waited for: 2 -> 2; matrix products, arithmetic and copies ran while one was open for 1% -> 9% of each run, Pallas kernels for 0% -> 0%
where the time goes in v1:
time: 114 us
  waiting for transfers between devices  53.2 us (47%)
  blocking collectives  17.4 us (15%)
  matrix products  14.4 us (13%)
  between operations  14.1 us (12%)
  starting transfers between devices  5.24 us (5%)
  local copies, waits for them, and re-layouts  5.07 us (4%)
  other arithmetic  4.32 us (4%)
    reduce_scatter x1, waiting for transfers between devices, body(): left_own = lax.psum_scatter(left, 'tensor', scatter_dimension=1, tiled=True)  28.8 us
    ppermute x2, waiting for transfers between devices, gather_around(): lower.append(lax.ppermute(lower[-1] if lower else x, axis, pairs))  24.3 us
    all_gather x1, blocking collectives, body(): block_decisions = lax.all_gather(query_decision, 'dp', axis=0, tiled=True)  10.9 us
    psum x1, blocking collectives, body(): result = lax.psum(partial_dec, ('tensor', 'layer'))  6.54 us
    dot_general x1, matrix products, body(): jnp.einsum('etf,fp->etp', hidden_rows, side_hidden, preferred_element_typ...  6.26 us
    gather x1, local copies, waits for them, and re-layouts, gather_around(): blocks = blocks[(jnp.arange(size) - shift) % size]  4.97 us
    another operation x1, other arithmetic, gather_around(): blocks = jnp.stack([*lower[::-1], x, *upper])  3.58 us
    dot_general x1, matrix products, body(): jnp.einsum('ek,qk->eq', grad_flat, block_rows, preferred_element_type=jnp...  3.37 us
  transfers between devices with their start and end apart: 5, of which 2 were waited for; matrix products, arithmetic and copies ran while one was open for 9% of the time, Pallas kernels for 0%

profile of v1, /device:TPU:0, one launch (start us, length us, event | category | flops | bytes accessed | tf_op | source)
XLA Modules:
  0.0 113.8 jit_solution(1224331434655017405)
XLA Ops:
  6.5 0.0 copy-start
  6.5 0.0 reduce-scatter.3.cloned.1.call-start
  6.5 0.0 copy-start.2
  6.5 0.0 copy-start.1
  6.5 3.1 %collective-permute-start = (bf16[256,2048]{1,0:T(8,128)(2,1)}, bf16[256,2048]{1,0:T(8,128)(2,1)}, u32[]{:S(2)}, u32[]{:S(2)}) collective-permute-start(bf16[256,2048]{1,0:T(8,128)(2,1)} %bitcast.46), channel_id=1, source_target_pairs={{0,4},{4,8},{8,12},{12,0},{1,5},{5,9},{9,13},{13,1},{2,6},{6,10},{... | collective-permute-start | bytes 3145736 | tf_op jit(solution)/shard_map/ppermute | solution.py:22
  9.7 2.1 %collective-permute-start.2 = (bf16[256,2048]{1,0:T(8,128)(2,1)}, bf16[256,2048]{1,0:T(8,128)(2,1)}, u32[]{:S(2)}, u32[]{:S(2)}) collective-permute-start(bf16[256,2048]{1,0:T(8,128)(2,1)} %bitcast.47), channel_id=1, source_target_pairs={{4,0},{8,4},{12,8},{0,12},{5,1},{9,5},{13,9},{1,13},{6,2},{10,6},{... | collective-permute-start | bytes 3145736 | tf_op jit(solution)/shard_map/ppermute | solution.py:24
  11.7 24.3 %collective-permute-done = bf16[256,2048]{1,0:T(8,128)(2,1)} collective-permute-done((bf16[256,2048]{1,0:T(8,128)(2,1)}, bf16[256,2048]{1,0:T(8,128)(2,1)}, u32[]{:S(2)}, u32[]{:S(2)}) %collective-permute-start) | collective-permute-done | bytes 1048608 | tf_op jit(solution)/shard_map/ppermute | solution.py:22
  36.1 0.0 collective-permute-start.1
  36.1 6.3 %fusion.9 = f32[1,512,64]{1,2,0:T(8,128)} fusion(bf16[1,1,512,7168]{3,2,1,0:T(8,128)(2,1)} %param.7, bf16[1,7168,64]{1,2,0:T(8,128)(2,1)} %param.9), kind=kOutput, calls=%fused_computation.10 | convolution fusion | flops 469762048 | bytes 8388608 | tf_op jit(solution)/shard_map/etf,fp->etp/dot_general | solution.py:50
  42.3 0.0 reduce-scatter.3.cloned.1.call-update
  42.3 0.0 reduce-scatter.5.cloned.1.call-start
  43.1 0.0 copy-done
  43.1 1.7 %fusion.12 = bf16[256,64]{1,0:T(8,128)(2,1)S(1)} fusion(bf16[1,1,256,4096]{3,2,1,0:T(8,128)(2,1)S(1)} %copy-done, bf16[1,4096,64]{1,2,0:T(8,128)(2,1)} %param.10, f32[256]{0:T(256)S(1)} %compare_convert_fusion), kind=kOutput, calls=%fused_computation.11 | convolution fusion | flops 134250496 | bytes 2655232 | tf_op jit(solution)/shard_map/etd,dp->etp/dot_general | solution.py:48
  44.8 28.8 %reduce-scatter.3.cloned.1.call-done = f32[1,256,64]{1,2,0:T(8,128)} async-done(((f32[1,512,64]{1,2,0:T(8,128)}), f32[1,256,64]{1,2,0:T(8,128)}) %reduce-scatter.3.cloned.1.call-update) | async-done | bytes 65552 | tf_op jit(solution)/shard_map/reduce_scatter | solution.py:51
  73.7 1.6 %fusion.15 = f32[1,64,64]{2,1,0:T(8,128)} fusion(bf16[256,64]{1,0:T(8,128)(2,1)S(1)} %fusion.12, f32[1,256,64]{1,2,0:T(8,128)} %reduce-scatter.3.cloned.1.call-done, f32[]{:T(128)} %bitcast.7), kind=kOutput, calls=%fused_computation.13 | convolution fusion | flops 12587008 | bytes 114692 | tf_op jit(solution)/shard_map/etp,etq->epq/dot_general | solution.py:52
  75.3 0.0 reduce-scatter.5.cloned.1.call-update
  75.3 0.0 copy-done.2
  75.3 10.9 %all-gather = s32[4,1,256]{2,1,0:T(1,128)S(1)} all-gather(s32[1,1,256]{2,1,0:T(1,128)S(1)} %bitcast.49), channel_id=1, replica_groups=mesh['groups'=2,'dp'=4,'tensor'=2,'layer'=2] {'dp'}, dimensions={0}, use_global_device_ids=true | all-gather | bytes 5120 | tf_op jit(solution)/shard_map/all_gather | solution.py:59
  86.2 0.0 reduce-scatter.5.cloned.1.call-done
  86.2 0.7 convert_element_type.30
  86.9 0.1 reshape.114
  87.0 0.0 collective-permute-done.2
  87.0 0.0 collective-permute-done.1
  87.0 0.0 copy-done.1
  87.0 3.6 %pad_maximum_fusion = bf16[4,256,2048]{2,1,0:T(8,128)(2,1)} fusion(bf16[1,256,2048]{2,1,0:T(8,128)(2,1)} %bitcast.12, bf16[1,256,2048]{2,1,0:T(8,128)(2,1)S(1)} %copy-done.1, bf16[1,256,2048]{2,1,0:T(8,128)(2,1)} %bitcast.11, bf16[1,256,2048]{2,1,0:T(8,128)(2,1)} %bitcast.10), kind=kLoop, calls=%fused_computation.3 | loop fusion | flops 6291456 | bytes 8388608 | tf_op jit(solution)/shard_map/stack | solution.py:25
  90.6 5.0 %gather_fusion = bf16[4,256,2048]{2,1,0:T(8,128)(2,1)} fusion(bf16[4,256,2048]{2,1,0:T(8,128)(2,1)} %pad_maximum_fusion, s32[1024]{0:T(1024)S(1)} %pad_clamp_fusion), kind=kCustom, calls=%fused_computation | custom fusion | bytes 8388624 | tf_op jit(solution)/shard_map/gather | solution.py:27
  95.6 3.4 %convolution_bitcast_fusion = f32[1024,1]{0,1:T(1,128)S(1)} fusion(bf16[2048,1]{0,1:T(2,128)(2,1)S(1)} %reshape.114, bf16[1024,2048]{1,0:T(8,128)(2,1)} %bitcast.45), kind=kOutput, calls=%fused_computation.14 | convolution fusion | flops 4194304 | bytes 4202496 | tf_op jit(solution)/shard_map/ek,qk->eq/dot_general | solution.py:60
  99.0 1.5 %fusion.2 = f32[1,1024]{1,0:T(1,128)S(1)} fusion(f32[1024,1]{0,1:T(1,128)S(1)} %convolution_bitcast_fusion, s32[1024]{0:T(1024)S(1)} %bitcast.48), kind=kOutput, calls=%fused_computation.5 | convolution fusion | flops 13631488 | bytes 12288 | tf_op jit(solution)/shard_map/dot_general | solution.py:61
  100.4 6.5 %psum.7 = f32[1,1024]{1,0:T(1,128)} all-reduce(f32[1,1024]{1,0:T(1,128)S(1)} %fusion.2), channel_id=1, replica_groups=mesh['groups'=2,'dp'=4,'tensor'=2,'layer'=2] {'tensor','layer'}, use_global_device_ids=true, to_apply=%region_2.3 | all-reduce | flops 1024 | bytes 8192 | tf_op jit(solution)/shard_map/psum | solution.py:62
  (3 shorter events, 0.0 us)
Async XLA Ops:
  6.5 36.5 %copy-start = (bf16[1,1,256,4096]{3,2,1,0:T(8,128)(2,1)S(1)}, bf16[1,1,256,4096]{3,2,1,0:T(8,128)(2,1)}, u32[]{:S(2)}) copy-start(bf16[1,1,256,4096]{3,2,1,0:T(8,128)(2,1)} %param.8) | copy-start | bytes 6291460
  6.5 67.1 %reduce-scatter.3.cloned.1.call-start = ((), (), s32[]{:S(2)}) async-start(), calls=%async_computation.2 | async-start | bytes 196608 | tf_op jit(solution)/shard_map/reduce_scatter | solution.py:51
  6.5 68.8 %copy-start.2 = (s32[256]{0:T(256)S(1)}, s32[256]{0:T(256)}, u32[]{:S(2)}) copy-start(s32[256]{0:T(256)} %param.13) | copy-start | bytes 3076
  6.5 80.5 %copy-start.1 = (bf16[1,256,2048]{2,1,0:T(8,128)(2,1)S(1)}, bf16[1,256,2048]{2,1,0:T(8,128)(2,1)}, u32[]{:S(2)}) copy-start(bf16[1,256,2048]{2,1,0:T(8,128)(2,1)} %param.11) | copy-start | bytes 3145732
  6.5 29.5 %collective-permute-start = (bf16[256,2048]{1,0:T(8,128)(2,1)}, bf16[256,2048]{1,0:T(8,128)(2,1)}, u32[]{:S(2)}, u32[]{:S(2)}) collective-permute-start(bf16[256,2048]{1,0:T(8,128)(2,1)} %bitcast.46), channel_id=1, source_target_pairs={{0,4},{4,8},{8,12},{12,0},{1,5},{5,9},{9,13},{13,1},{2,6},{6,10},{... | collective-permute-start | bytes 3145736 | tf_op jit(solution)/shard_map/ppermute | solution.py:22
  9.7 77.4 %collective-permute-start.2 = (bf16[256,2048]{1,0:T(8,128)(2,1)}, bf16[256,2048]{1,0:T(8,128)(2,1)}, u32[]{:S(2)}, u32[]{:S(2)}) collective-permute-start(bf16[256,2048]{1,0:T(8,128)(2,1)} %bitcast.47), channel_id=1, source_target_pairs={{4,0},{8,4},{12,8},{0,12},{5,1},{9,5},{13,9},{1,13},{6,2},{10,6},{... | collective-permute-start | bytes 3145736 | tf_op jit(solution)/shard_map/ppermute | solution.py:24
  36.1 51.0 %collective-permute-start.1 = (bf16[256,2048]{1,0:T(8,128)(2,1)}, bf16[256,2048]{1,0:T(8,128)(2,1)}, u32[]{:S(2)}, u32[]{:S(2)}) collective-permute-start(bf16[256,2048]{1,0:T(8,128)(2,1)} %collective-permute-done), channel_id=1, source_target_pairs={{0,4},{4,8},{8,12},{12,0},{1,5},{5,9},{9,13},{13,1},{2,6},{6,10},{... | collective-permute-start | bytes 3145736 | tf_op jit(solution)/shard_map/ppermute | solution.py:22
  42.3 43.9 %reduce-scatter.5.cloned.1.call-start = ((), (), s32[]{:S(2)}) async-start(), calls=%async_computation.3 | async-start | bytes 49152 | tf_op jit(solution)/shard_map/reduce_scatter | solution.py:56
Sparse Core Ops, SparseCore 0:
  42.5 31.1 reduce-scatter.2
  75.8 9.9 reduce-scatter.4
